TPU v7x, 128 devices: a whole 4x4x4 slice. The times are simulated.
128 devices in a mesh: dp: 16 (over x, y_hi, core), tensor: 8 (over y_lo, z).
Axes of the slice: x: 4, y: 4 (y_hi: 2, y_lo: 2; y = y_hi * 2 + y_lo), z: 4, core: 2. Of those that a mesh axis runs over, the one named last changes fastest.
Arguments:
- hidden_state_input: bfloat16 [16384, 3584], P(('dp', 'tensor')), may hold values from -500 to 500
- token_embedding_input: bfloat16 [16384, 3584], P(('dp', 'tensor')), may hold values from -500 to 500
- input_norm_gain: float32 [7168], replicated, may hold values from 0.1 to 1.9
- query_projection_weight: bfloat16 [7168, 3584], P('dp', 'tensor'), may hold values from -0.0625 to 0.0625
- key_projection_weight: bfloat16 [7168, 3584], P('dp', 'tensor'), may hold values from -0.0625 to 0.0625
- value_projection_weight: bfloat16 [7168, 3584], P('dp', 'tensor'), may hold values from -0.0625 to 0.0625
- adapter_down_maps: bfloat16 [7168, 384], replicated, may hold values from -1 to 1
- adapter_up_maps: bfloat16 [3, 128, 3584], P(None, None, 'tensor'), may hold values from -2 to 2
- output_projection_weight: bfloat16 [3584, 3584], P('tensor'), may hold values from -0.09375 to 0.09375
- segment: int32 [16384], P('dp'), may hold values from 0 to 3, as said below
- live_token_length: int32 [16], P('dp'), may hold values from 512 to 1024, as said below
- request_cache_row: int32 [64], P('dp'), may hold values from 0 to 63, as said below
Outputs:
- block_out: bfloat16 [16384, 3584], P(('dp', 'tensor'))
- kv_cache: bfloat16 [64, 256, 2, 3584], P(None, 'dp', None, 'tensor')
Inputs may be any that keep to these rules, and one draw needn't show every extreme that they name: `segment`: within a stream, the live slots carry request numbers that never fall, every request 0 to 3 appears, each on (257) // 2 to 256 slots, some request in every draw on exactly 256; slots at or past live_token_length hold 3. `live_token_length`: each stream's live tokens; some stream is full in every draw. `request_cache_row`: A permutation of the 64 cache rows.
All inputs are finite; a program needn't handle non-finite values.
Results may differ from a plain program's by a relative error of at most 0.015.
The roundings to bfloat16 on the way count: a program that leaves them out, or rounds other values in their place, can miss the bound.
Values may be sent and summed in bfloat16 or wider, within the bound.
No kernel may reach another device: no remote copies, remote signals or barrier semaphores. Data moves between devices by JAX's collectives and lax.ppermute only.
A program may use at most 128 MiB of HBM per device.

v0:
```python
import math
import jax
import jax.numpy as jnp
from jax import lax
from jax.sharding import PartitionSpec as P

HD = 224
epsilon = 1e-05
negative = -1e30


def normalize(hidden_state_input, token_embedding_input, input_norm_gain):
    combined = jnp.concatenate([hidden_state_input, token_embedding_input], 1).astype(jnp.float32)
    factor = lax.rsqrt(jnp.mean(combined * combined, axis=1, keepdims=True) + epsilon)
    return (combined * factor * input_norm_gain).astype(jnp.bfloat16)


def attend_block(query, keys, values, segment, position, live, first, count, key_end):
    heads = query.shape[1] // HD
    block_query = query[first : first + count].reshape(count, heads, HD)
    block_keys = keys.reshape(key_end, heads, HD)
    block_values = values.reshape(key_end, heads, HD)
    scores = jnp.einsum(
        "qhd,khd->hqk", block_query, block_keys, preferred_element_type=jnp.float32
    ) / math.sqrt(HD)
    query_at = position[first : first + count]
    allowed = (
        (segment[first : first + count, None] == segment[None, :key_end])
        & (position[None, :] <= query_at[:, None])
        & (position[None, :] < live)
    )
    scores = jnp.where(allowed[None], scores, negative)
    top = jnp.max(scores, axis=-1, keepdims=True)
    expo = jnp.exp(scores - top)
    weights = (expo / jnp.sum(expo, axis=-1, keepdims=True)).astype(jnp.bfloat16)
    mixed = jnp.einsum("hqk,khd->qhd", weights, block_values, preferred_element_type=jnp.float32)
    mixed = jnp.where((query_at < live)[:, None, None], mixed, 0.0)
    return mixed.astype(jnp.bfloat16).reshape(count, heads * HD)


def body(
    hidden_state_input,
    token_embedding_input,
    input_norm_gain,
    query_projection_weight,
    key_projection_weight,
    value_projection_weight,
    adapter_down_maps,
    adapter_up_maps,
    output_projection_weight,
    segment,
    live_token_length,
    request_cache_row,
):
    adapter_rank_width = adapter_up_maps.shape[1]
    head_cols = query_projection_weight.shape[1]
    normalized_hidden = normalize(hidden_state_input, token_embedding_input, input_norm_gain)
    adapter_update = jnp.dot(
        normalized_hidden, adapter_down_maps, preferred_element_type=jnp.float32
    ).astype(jnp.bfloat16)
    stream_in, stream_low = (
        lax.all_gather(normalized_hidden, "tensor", axis=0, tiled=True),
        lax.all_gather(adapter_update, "tensor", axis=0, tiled=True),
    )
    pieces = (
        lax.all_gather(query_projection_weight, "dp", axis=0, tiled=True),
        lax.all_gather(key_projection_weight, "dp", axis=0, tiled=True),
        lax.all_gather(value_projection_weight, "dp", axis=0, tiled=True),
    )
    folded = tuple(
        (jnp.dot(stream_in, piece, preferred_element_type=jnp.float32) for piece in pieces)
    )
    projected = []
    for adapter_selector in range(3):
        adapter = jnp.dot(
            stream_low[
                :,
                adapter_selector * adapter_rank_width : (adapter_selector + 1) * adapter_rank_width,
            ],
            adapter_up_maps[adapter_selector],
            preferred_element_type=jnp.float32,
        )
        projected.append((folded[adapter_selector] + adapter).astype(jnp.bfloat16))
    query, keys, values = projected
    stream = query.shape[0]
    position = jnp.arange(stream, dtype=jnp.int32)
    live = live_token_length[0]
    block = min(512, stream)
    attended_parts = []
    for block_index in range(stream // block):
        first = block_index * block
        attended_parts.append(
            attend_block(query, keys, values, segment, position, live, first, block, stream)
        )
    attended = jnp.concatenate(attended_parts, 0)
    block_out = lax.psum_scatter(
        jnp.dot(attended, output_projection_weight, preferred_element_type=jnp.float32).astype(
            jnp.bfloat16
        ),
        "tensor",
        scatter_dimension=0,
        tiled=True,
    )
    requests = request_cache_row.shape[0]
    longest = stream // requests
    groups = lax.axis_size("dp")
    piece_len = longest // groups
    numbers = jnp.arange(requests, dtype=jnp.int32)
    membership = ((segment[:, None] == numbers[None, :]) & (position < live)[:, None]).astype(
        jnp.int32
    )
    lengths = jnp.sum(membership, axis=0)
    starts = jnp.cumsum(lengths) - lengths
    offsets = (
        jnp.arange(groups, dtype=jnp.int32)[:, None] * piece_len
        + jnp.arange(piece_len, dtype=jnp.int32)[None, :]
    )
    source_rows = jnp.minimum(starts[None, :, None] + offsets[:, None, :], stream - 1)
    alive_mask = offsets[:, None, :] < lengths[None, :, None]
    stacked = jnp.stack([keys, values], 1).reshape(stream, 2 * head_cols)
    taken = jnp.take(stacked, source_rows.reshape(-1), axis=0)
    taken = jnp.where(alive_mask.reshape(-1)[:, None], taken, jnp.zeros((), jnp.bfloat16))
    taken = taken.reshape(groups, requests, piece_len * 2 * head_cols)
    row_send = jnp.broadcast_to(request_cache_row[None, :], (groups, requests))
    received, received_rows = (
        lax.all_to_all(taken, "dp", split_axis=0, concat_axis=0, tiled=True),
        lax.all_to_all(row_send, "dp", split_axis=0, concat_axis=0, tiled=True),
    )
    total_reqs = groups * requests
    placing = (
        received_rows.reshape(-1)[:, None] == jnp.arange(total_reqs, dtype=jnp.int32)[None, :]
    ).astype(jnp.bfloat16)
    flat_received = received.reshape(total_reqs, piece_len * 2 * head_cols)
    cache_rows = lax.dot_general(
        placing, flat_received, (((0,), (0,)), ((), ())), preferred_element_type=jnp.float32
    )
    kv_cache = cache_rows.astype(jnp.bfloat16).reshape(total_reqs, piece_len, 2, head_cols)
    return (block_out, kv_cache)


def solution(mesh):
    return jax.shard_map(
        body,
        mesh=mesh,
        in_specs=(
            P(("dp", "tensor"), None),
            P(("dp", "tensor"), None),
            P(),
            P("dp", "tensor"),
            P("dp", "tensor"),
            P("dp", "tensor"),
            P(),
            P(None, None, "tensor"),
            P("tensor", None),
            P("dp"),
            P("dp"),
            P("dp"),
        ),
        out_specs=(P(("dp", "tensor"), None), P(None, "dp", None, "tensor")),
        check_vma=False,
    )
```

profile of v0, /device:TPU:1, one launch (start us, length us, event | category | flops | bytes accessed | tf_op | source)
XLA Modules:
  0.0 503.1 jit_solution(3945014618020465741)
XLA Ops:
  15.4 4.3 convolution_convert_fusion.2
  19.7 28.2 %all_gather.17 = bf16[1024,384]{1,0:T(8,128)(2,1)S(1)} all-gather(bf16[128,384]{1,0:T(8,128)(2,1)S(1)} %convolution_convert_fusion.2), channel_id=1, replica_groups=mesh['dp'=16,'tensor'=8] {'tensor'}, dimensions={0}, use_global_device_ids=true | all-gather | bytes 884736 | tf_op jit(solution)/shard_map/all_gather | solution.py:63
  55.1 27.7 %all-gather.9.cloned.1.call-done = bf16[7168,448]{1,0:T(8,128)(2,1)} async-done(((bf16[448,448]{1,0:T(8,128)(2,1)}), bf16[7168,448]{1,0:T(8,128)(2,1)}) %all-gather.9.cloned.1.call-update) | async-done | bytes 6422544 | tf_op jit(solution)/shard_map/all_gather | solution.py:66
  82.9 150.3 %all-gather.5.cloned.1.call-done = bf16[1024,7168]{1,0:T(8,128)(2,1)} async-done(((bf16[128,7168]{1,0:T(8,128)(2,1)}), bf16[1024,7168]{1,0:T(8,128)(2,1)}) %all-gather.5.cloned.1.call-update) | async-done | bytes 14680080 | tf_op jit(solution)/shard_map/all_gather | solution.py:62
  233.2 13.3 %add_convert_fusion.1 = bf16[1024,448]{0,1:T(8,128)(2,1)} fusion(f32[1024,448]{0,1:T(8,128)} %fusion.28, bf16[1024,7168]{1,0:T(8,128)(2,1)} %all-gather.5.cloned.1.call-done, bf16[7168,448]{1,0:T(8,128)(2,1)} %all-gather.9.cloned.1.call-done), kind=kOutput, calls=%fused_computation.36 | convolution fusion | flops 6577586176 | bytes 23855104 | tf_op jit(solution)/shard_map/dot_general | solution.py:71
  248.6 54.5 %all-gather.11.cloned.1.call-done = bf16[7168,448]{1,0:T(8,128)(2,1)} async-done(((bf16[448,448]{1,0:T(8,128)(2,1)}), bf16[7168,448]{1,0:T(8,128)(2,1)}) %all-gather.11.cloned.1.call-update) | async-done | bytes 6422544 | tf_op jit(solution)/shard_map/all_gather | solution.py:67
  303.1 13.3 %add_convert_fusion = bf16[1024,448]{0,1:T(8,128)(2,1)} fusion(f32[1024,448]{0,1:T(8,128)} %fusion.26, bf16[1024,7168]{1,0:T(8,128)(2,1)} %all-gather.5.cloned.1.call-done, bf16[7168,448]{1,0:T(8,128)(2,1)} %all-gather.11.cloned.1.call-done), kind=kOutput, calls=%fused_computation.35 | convolution fusion | flops 6577586176 | bytes 23855104 | tf_op jit(solution)/shard_map/dot_general | solution.py:71
  316.4 5.2 %fusion.51 = (f32[2,512]{1,0:T(2,128)S(1)}, f32[2,512,1024]{2,1,0:T(8,128)}) fusion(pred[512,1024]{1,0:T(8,128)(4,1)} %get-tuple-element.7, bf16[512,2,224]{0,2,1:T(8,128)(2,1)} %bitcast.61, bf16[1024,2,224]{0,2,1:T(8,128)(2,1)} %bitcast.54), kind=kOutput, calls=%fused_computation.85 | convolution fusion | flops 473957376 | bytes 6098944 | tf_op jit(solution)/shard_map/sub | solution.py:34
  321.6 5.3 %fusion.52 = (f32[2,512]{1,0:T(2,128)S(1)}, f32[2,512,1024]{2,1,0:T(8,128)}) fusion(pred[512,1024]{1,0:T(8,128)(4,1)} %get-tuple-element.6, bf16[512,2,224]{0,2,1:T(8,128)(2,1)} %bitcast.60, bf16[1024,2,224]{0,2,1:T(8,128)(2,1)} %bitcast.55), kind=kOutput, calls=%fused_computation.86 | convolution fusion | flops 473957376 | bytes 6098944 | tf_op jit(solution)/shard_map/sub | solution.py:34
  326.9 44.8 %all-gather.7.cloned.1.call-done = bf16[7168,448]{1,0:T(8,128)(2,1)} async-done(((bf16[448,448]{1,0:T(8,128)(2,1)}), bf16[7168,448]{1,0:T(8,128)(2,1)}) %all-gather.7.cloned.1.call-update) | async-done | bytes 6422544 | tf_op jit(solution)/shard_map/all_gather | solution.py:68
  371.7 13.3 %add_convert_fusion.2 = bf16[1024,448]{0,1:T(8,128)(2,1)} fusion(f32[1024,448]{0,1:T(8,128)} %fusion.30, bf16[1024,7168]{1,0:T(8,128)(2,1)} %all-gather.5.cloned.1.call-done, bf16[7168,448]{1,0:T(8,128)(2,1)} %all-gather.7.cloned.1.call-done), kind=kOutput, calls=%fused_computation.37 | convolution fusion | flops 6577586176 | bytes 23855104 | tf_op jit(solution)/shard_map/dot_general | solution.py:71
  390.0 6.1 %convolution_convert_fusion.1 = bf16[1024,3584]{1,0:T(8,128)(2,1)} fusion(bf16[448,3584]{1,0:T(8,128)(2,1)S(1)} %copy-done, bf16[512,448]{0,1:T(8,128)(2,1)S(1)} %bitcast.64, bf16[512,448]{0,1:T(8,128)(2,1)S(1)} %bitcast.65), kind=kOutput, calls=%fused_computation.4 | convolution fusion | flops 3293839360 | bytes 11468800 | tf_op jit(solution)/shard_map/dot_general | solution.py:97
  397.3 3.6 all-to-all-start
  402.7 4.0 broadcast_in_dim.106
  407.9 3.9 broadcast_in_dim.108
  414.9 3.9 copy.17
  418.8 7.5 %gather_fusion = bf16[1024,896]{1,0:T(8,128)(2,1)} fusion(bf16[1024,896]{1,0:T(8,128)(2,1)} %copy.17, s32[1024]{0:T(1024)S(1)} %broadcast_clamp_fusion), kind=kCustom, calls=%fused_computation | custom fusion | bytes 3674112 | tf_op jit(solution)/shard_map/jit(_take)/gather | solution.py:121
  426.3 4.4 gather.7
  430.6 5.5 %select_select_fusion = bf16[16,4,14336]{2,1,0:T(4,128)(2,1)} fusion(pred[16,4,14336]{2,1,0:T(4,128)(4,1)} %broadcast_in_dim.106, pred[16,4,14336]{2,1,0:T(4,128)(4,1)} %broadcast_in_dim.108, bf16[16,4,14336]{2,1,0:T(4,128)(2,1)} %gather.7), kind=kLoop, calls=%fused_computation.34 | loop fusion | flops 1835008 | bytes 5505024 | tf_op jit(solution)/shard_map/jit(_where)/select_n | solution.py:122
  436.2 7.1 %all-to-all-start.1 = ((bf16[16,4,14336]{2,1,0:T(4,128)(2,1)}), bf16[16,4,14336]{2,1,0:T(4,128)(2,1)}, u32[]{:S(2)}, u32[]{:S(2)}) async-start(bf16[16,4,14336]{2,1,0:T(4,128)(2,1)} %select_select_fusion), calls=%async_computation.2 | async-start | bytes 3670016 | tf_op jit(solution)/shard_map/all_to_all | solution.py:126
  444.5 28.2 %all-to-all-done.1 = bf16[16,4,14336]{2,1,0:T(4,128)(2,1)} async-done(((bf16[16,4,14336]{2,1,0:T(4,128)(2,1)}), bf16[16,4,14336]{2,1,0:T(4,128)(2,1)}, u32[]{:S(2)}, u32[]{:S(2)}) %all-to-all-start.1) | async-done | bytes 1835040 | tf_op jit(solution)/shard_map/all_to_all | solution.py:126
  472.7 3.9 reshape.308
  480.1 6.8 %reshape.309 = bf16[64,16,2,448]{3,2,1,0:T(2,128)(2,1)} reshape(bf16[64,14336]{1,0:T(8,128)(2,1)} %convolution_convert_fusion) | data formatting | bytes 3670016 | tf_op jit(solution)/shard_map/reshape | solution.py:137
  486.9 9.7 %reduce-scatter.2.cloned.1.call-done = bf16[128,3584]{1,0:T(8,128)(2,1)} async-done(((bf16[1024,3584]{1,0:T(8,128)(2,1)}), bf16[128,3584]{1,0:T(8,128)(2,1)}) %reduce-scatter.2.cloned.1.call-update) | async-done | bytes 917520 | tf_op jit(solution)/shard_map/reduce_scatter | solution.py:96
  (61 shorter events, 33.8 us)
Async XLA Ops:
  7.2 382.8 %copy-start = (bf16[448,3584]{1,0:T(8,128)(2,1)S(1)}, bf16[448,3584]{1,0:T(8,128)(2,1)}, u32[]{:S(2)}) copy-start(bf16[448,3584]{1,0:T(8,128)(2,1)} %param.20) | copy-start | bytes 9633796
  7.2 75.7 %all-gather.9.cloned.1.call-start = ((), (), s32[]{:S(2)}) async-start(), calls=%async_computation.5 | async-start | bytes 7798784 | tf_op jit(solution)/shard_map/all_gather | solution.py:66
  7.9 225.2 %all-gather.5.cloned.1.call-start = ((), (), s32[]{:S(2)}) async-start(), calls=%async_computation.3 | async-start | bytes 16515072 | tf_op jit(solution)/shard_map/all_gather | solution.py:62
  10.0 5.3 %copy-start.3 = (s32[1024]{0:T(1024)S(1)}, s32[1024]{0:T(1024)}, u32[]{:S(2)}) copy-start(s32[1024]{0:T(1024)} %param.21) | copy-start | bytes 12292
  13.3 289.8 %all-gather.11.cloned.1.call-start = ((), (), s32[]{:S(2)}) async-start(), calls=%async_computation.6 | async-start | bytes 7798784 | tf_op jit(solution)/shard_map/all_gather | solution.py:67
  14.0 357.7 %all-gather.7.cloned.1.call-start = ((), (), s32[]{:S(2)}) async-start(), calls=%async_computation.4 | async-start | bytes 7798784 | tf_op jit(solution)/shard_map/all_gather | solution.py:68
  14.6 482.0 %reduce-scatter.2.cloned.1.call-start = ((), (), s32[]{:S(2)}) async-start(), calls=%async_computation.7 | async-start | bytes 8257536 | tf_op jit(solution)/shard_map/reduce_scatter | solution.py:96
  14.7 5.0 %copy-start.4 = (s32[1024]{0:T(1024)}, s32[1024]{0:T(1024)S(1)}, u32[]{:S(2)}) copy-start(s32[1024]{0:T(1024)S(1)} %iota.48) | copy-start | bytes 12292
  15.4 32.5 %copy-start.2 = (bf16[3,128,448]{1,2,0:T(8,128)(2,1)S(1)}, bf16[3,128,448]{1,2,0:T(8,128)(2,1)}, u32[]{:S(2)}) copy-start(bf16[3,128,448]{1,2,0:T(8,128)(2,1)} %param.19) | copy-start | bytes 1032196
  47.9 5.0 %slice-start = ((s32[1024]{0:T(1024)}), s32[512]{0:T(512)S(1)}, s32[]{:S(2)}) async-start(s32[1024]{0:T(1024)} %copy-done.4), calls=%async_computation.8 | async-start | bytes 4096 | tf_op jit(solution)/shard_map/slice | solution.py:26
  385.0 3.5 copy-start.1
  385.0 4.0 copy-start.6
  396.1 0.7 copy-start.5
  397.3 38.9 %all-to-all-start = ((s32[16,1,4]{2,1,0:T(1,128)}), s32[16,1,4]{2,1,0:T(1,128)S(1)}, u32[]{:S(2)}, u32[]{:S(2)}) async-start(s32[16,1,4]{2,1,0:T(1,128)} %broadcast_in_dim.104), calls=%async_computation.1 | async-start | bytes 16384 | tf_op jit(solution)/shard_map/all_to_all | solution.py:127
  436.2 36.5 %all-to-all-start.1 = ((bf16[16,4,14336]{2,1,0:T(4,128)(2,1)}), bf16[16,4,14336]{2,1,0:T(4,128)(2,1)}, u32[]{:S(2)}, u32[]{:S(2)}) async-start(bf16[16,4,14336]{2,1,0:T(4,128)(2,1)} %select_select_fusion), calls=%async_computation.2 | async-start | bytes 3670016 | tf_op jit(solution)/shard_map/all_to_all | solution.py:126
Sparse Core Ops, SparseCore 0:
  10.4 72.4 all-gather.8
  85.1 148.0 all-gather.4
  235.6 67.4 all-gather.10
  305.3 66.3 all-gather.6
  396.2 100.3 reduce-scatter.1
where the time goes:
time: 504 us; the launch traced here: 503 us
  waiting for transfers between devices  317 us (63%)
  matrix products  73.9 us (15%)
  local copies, waits for them, and re-layouts  41.3 us (8%)
  blocking collectives  28.2 us (6%)
  other arithmetic  17.1 us (3%)
  between operations  14.6 us (3%)
  starting transfers between devices  10.9 us (2%)
    all_gather x1, waiting for transfers between devices, body(): lax.all_gather(normalized_hidden, 'tensor', axis=0, tiled=True)  150 us
    all_gather x1, waiting for transfers between devices, body(): lax.all_gather(key_projection_weight, 'dp', axis=0, tiled=True)  54.5 us
    all_gather x1, waiting for transfers between devices, body(): lax.all_gather(value_projection_weight, 'dp', axis=0, tiled=True)  44.8 us
    dot_general x3, matrix products, body(): jnp.dot(stream_in, piece, preferred_element_type=jnp.float32)  39.9 us
    all_gather x1, blocking collectives, body(): lax.all_gather(adapter_update, 'tensor', axis=0, tiled=True)  28.2 us
    all_to_all x1, waiting for transfers between devices, body(): lax.all_to_all(taken, 'dp', split_axis=0, concat_axis=0, tiled=True)  28.2 us
    all_gather x1, waiting for transfers between devices, body(): lax.all_gather(query_projection_weight, 'dp', axis=0, tiled=True)  27.7 us
    gather x2, local copies, waits for them, and re-layouts, body(): taken = jnp.take(stacked, source_rows.reshape(-1), axis=0)  11.8 us
  transfers between devices with their start and end apart: 7, of which 6 were waited for; matrix products, arithmetic and copies ran while one was open for 21% of the time, Pallas kernels for 0%

commit v1 on v0

--- a/solution.py
+++ b/solution.py
@@ -59,7 +59,12 @@
         normalized_hidden, adapter_down_maps, preferred_element_type=jnp.float32
     ).astype(jnp.bfloat16)
     stream_in, stream_low = (
-        lax.all_gather(normalized_hidden, "tensor", axis=0, tiled=True),
+        jnp.concatenate(
+            lax.all_to_all(
+                jnp.stack([normalized_hidden] * lax.axis_size("tensor")), "tensor", 0, 0
+            ),
+            axis=0,
+        ),
         lax.all_gather(adapter_update, "tensor", axis=0, tiled=True),
     )
     pieces = (

time: 504 us -> 451 us (0.89)
  waiting for transfers between devices: 317 us -> 37.5 us
  blocking collectives: 28.2 us -> 235 us
  starting transfers between devices: 10.9 us -> 25.7 us
  local copies, waits for them, and re-layouts: 41.3 us -> 47.8 us
    all_gather x1, blocking collectives: 28.2 us -> 235 us  [body(): lax.all_gather(adapter_update, 'tensor', axis=0, tiled=True)]
    all_gather x1 -> x0, waiting for transfers between devices: 150 us -> none  [body(): lax.all_gather(normalized_hidden, 'tensor', axis=0, tiled=True)]
    all_gather x1, waiting for transfers between devices: 54.5 us -> 0.01 us  [body(): lax.all_gather(key_projection_weight, 'dp', axis=0, tiled=True)]
    all_gather x1, waiting for transfers between devices: 44.8 us -> 0.01 us  [body(): lax.all_gather(value_projection_weight, 'dp', axis=0, tiled=True)]
    all_gather x1, waiting for transfers between devices: 27.7 us -> 0.01 us  [body(): lax.all_gather(query_projection_weight, 'dp', axis=0, tiled=True)]
    all_to_all x1, starting transfers between devices: 3.63 us -> 11.4 us  [body(): lax.all_to_all(row_send, 'dp', split_axis=0, concat_axis=0, tiled=True)]
    all_to_all x0 -> x1, starting transfers between devices: none -> 7 us  [body(): lax.all_to_all(jnp.stack([normalized_hidden] * lax.axis_size('tensor')),...]
    another operation x0 -> x1, local copies, waits for them, and re-layouts: none -> 5.42 us  [body(): jnp.stack([normalized_hidden] * lax.axis_size('tensor'))]
  transfers between devices with their start and end apart: 7 -> 7, of which waited for: 6 -> 2; matrix products, arithmetic and copies ran while one was open for 21% -> 25% of each run, Pallas kernels for 0% -> 0%
where the time goes in v1:
time: 451 us; the launch traced here: 450 us
  blocking collectives  235 us (52%)
  matrix products  74 us (16%)
  local copies, waits for them, and re-layouts  47.8 us (11%)
  waiting for transfers between devices  37.5 us (8%)
  starting transfers between devices  25.7 us (6%)
  other arithmetic  15.7 us (3%)
  between operations  14.6 us (3%)
    all_gather x1, blocking collectives, body(): lax.all_gather(adapter_update, 'tensor', axis=0, tiled=True)  235 us
    dot_general x3, matrix products, body(): jnp.dot(stream_in, piece, preferred_element_type=jnp.float32)  40.2 us
    all_to_all x1, waiting for transfers between devices, body(): lax.all_to_all(taken, 'dp', split_axis=0, concat_axis=0, tiled=True)  28.2 us
    gather x2, local copies, waits for them, and re-layouts, body(): taken = jnp.take(stacked, source_rows.reshape(-1), axis=0)  11.8 us
    all_to_all x1, starting transfers between devices, body(): lax.all_to_all(row_send, 'dp', split_axis=0, concat_axis=0, tiled=True)  11.4 us
    sub x2, matrix products, attend_block(): expo = jnp.exp(scores - top)  10.4 us
  transfers between devices with their start and end apart: 7, of which 2 were waited for; matrix products, arithmetic and copies ran while one was open for 25% of the time, Pallas kernels for 0%

profile of v1, /device:TPU:1, one launch (start us, length us, event | category | flops | bytes accessed | tf_op | source)
XLA Modules:
  0.0 450.3 jit_solution(7386189608324522089)
XLA Ops:
  13.8 5.4 %stack.8 = bf16[8,128,7168]{2,1,0:T(8,128)(2,1)} broadcast(bf16[128,7168]{1,0:T(8,128)(2,1)S(1)} %fusion.4), dimensions={1,2} | broadcast | bytes 16515072 | tf_op jit(solution)/shard_map/stack | solution.py:64
  19.2 7.0 %all-to-all-start = ((bf16[8,128,7168]{2,1,0:T(8,128)(2,1)}), bf16[8,128,7168]{2,1,0:T(8,128)(2,1)}, u32[]{:S(2)}, u32[]{:S(2)}) async-start(bf16[8,128,7168]{2,1,0:T(8,128)(2,1)} %stack.8), calls=%async_computation | async-start | bytes 29360128 | tf_op jit(solution)/shard_map/all_to_all | solution.py:63
  27.8 4.3 convolution_convert_fusion.2
  32.1 234.9 %all_gather.13 = bf16[1024,384]{1,0:T(8,128)(2,1)S(1)} all-gather(bf16[128,384]{1,0:T(8,128)(2,1)S(1)} %convolution_convert_fusion.2), channel_id=1, replica_groups=mesh['dp'=16,'tensor'=8] {'tensor'}, dimensions={0}, use_global_device_ids=true | all-gather | bytes 884736 | tf_op jit(solution)/shard_map/all_gather | solution.py:68
  274.1 13.3 %add_convert_fusion.1 = bf16[1024,448]{0,1:T(8,128)(2,1)} fusion(f32[1024,448]{0,1:T(8,128)} %fusion.28, bf16[1024,7168]{1,0:T(8,128)(2,1)} %bitcast.1, bf16[7168,448]{1,0:T(8,128)(2,1)} %all-gather.6.cloned.1.call-done), kind=kOutput, calls=%fused_computation.36 | convolution fusion | flops 6577586176 | bytes 23855104 | tf_op jit(solution)/shard_map/dot_general | solution.py:76
  289.5 13.3 %add_convert_fusion = bf16[1024,448]{0,1:T(8,128)(2,1)} fusion(f32[1024,448]{0,1:T(8,128)} %fusion.26, bf16[1024,7168]{1,0:T(8,128)(2,1)} %bitcast.1, bf16[7168,448]{1,0:T(8,128)(2,1)} %all-gather.8.cloned.1.call-done), kind=kOutput, calls=%fused_computation.35 | convolution fusion | flops 6577586176 | bytes 23855104 | tf_op jit(solution)/shard_map/dot_general | solution.py:76
  302.9 5.2 %fusion.52 = (f32[2,512]{1,0:T(2,128)S(1)}, f32[2,512,1024]{2,1,0:T(8,128)}) fusion(pred[512,1024]{1,0:T(8,128)(4,1)} %get-tuple-element.6, bf16[512,2,224]{0,2,1:T(8,128)(2,1)} %bitcast.62, bf16[1024,2,224]{0,2,1:T(8,128)(2,1)} %bitcast.55), kind=kOutput, calls=%fused_computation.86 | convolution fusion | flops 473957376 | bytes 6098944 | tf_op jit(solution)/shard_map/sub | solution.py:34
  308.0 5.3 %fusion.51 = (f32[2,512]{1,0:T(2,128)S(1)}, f32[2,512,1024]{2,1,0:T(8,128)}) fusion(pred[512,1024]{1,0:T(8,128)(4,1)} %get-tuple-element.7, bf16[512,2,224]{0,2,1:T(8,128)(2,1)} %bitcast.61, bf16[1024,2,224]{0,2,1:T(8,128)(2,1)} %bitcast.56), kind=kOutput, calls=%fused_computation.85 | convolution fusion | flops 473957376 | bytes 6098944 | tf_op jit(solution)/shard_map/sub | solution.py:34
  313.3 13.5 %add_convert_fusion.2 = bf16[1024,448]{0,1:T(8,128)(2,1)} fusion(f32[1024,448]{0,1:T(8,128)} %fusion.30, bf16[1024,7168]{1,0:T(8,128)(2,1)} %bitcast.1, bf16[7168,448]{1,0:T(8,128)(2,1)} %all-gather.4.cloned.1.call-done), kind=kOutput, calls=%fused_computation.37 | convolution fusion | flops 6577586176 | bytes 23855104 | tf_op jit(solution)/shard_map/dot_general | solution.py:76
  326.8 3.5 fusion.22
  331.7 6.1 %convolution_convert_fusion.1 = bf16[1024,3584]{1,0:T(8,128)(2,1)} fusion(bf16[448,3584]{1,0:T(8,128)(2,1)S(1)} %copy-done, bf16[512,448]{0,1:T(8,128)(2,1)S(1)} %bitcast.66, bf16[512,448]{0,1:T(8,128)(2,1)S(1)} %bitcast.65), kind=kOutput, calls=%fused_computation.4 | convolution fusion | flops 3293839360 | bytes 11468800 | tf_op jit(solution)/shard_map/dot_general | solution.py:102
  339.1 11.4 %all-to-all-start.1 = ((s32[16,1,4]{2,1,0:T(1,128)}), s32[16,1,4]{2,1,0:T(1,128)S(1)}, u32[]{:S(2)}, u32[]{:S(2)}) async-start(s32[16,1,4]{2,1,0:T(1,128)} %broadcast_in_dim.104), calls=%async_computation.2 | async-start | bytes 16384 | tf_op jit(solution)/shard_map/all_to_all | solution.py:132
  352.4 3.9 broadcast_in_dim.106
  357.5 3.9 broadcast_in_dim.108
  364.4 3.9 copy.17
  368.3 7.5 %gather_fusion = bf16[1024,896]{1,0:T(8,128)(2,1)} fusion(bf16[1024,896]{1,0:T(8,128)(2,1)} %copy.17, s32[1024]{0:T(1024)S(1)} %broadcast_clamp_fusion), kind=kCustom, calls=%fused_computation | custom fusion | bytes 3674112 | tf_op jit(solution)/shard_map/jit(_take)/gather | solution.py:126
  375.7 4.4 gather.7
  380.1 5.5 %select_select_fusion = bf16[16,4,14336]{2,1,0:T(4,128)(2,1)} fusion(pred[16,4,14336]{2,1,0:T(4,128)(4,1)} %broadcast_in_dim.106, pred[16,4,14336]{2,1,0:T(4,128)(4,1)} %broadcast_in_dim.108, bf16[16,4,14336]{2,1,0:T(4,128)(2,1)} %gather.7), kind=kLoop, calls=%fused_computation.34 | loop fusion | flops 1835008 | bytes 5505024 | tf_op jit(solution)/shard_map/jit(_where)/select_n | solution.py:127
  385.6 7.2 %all-to-all-start.2 = ((bf16[16,4,14336]{2,1,0:T(4,128)(2,1)}), bf16[16,4,14336]{2,1,0:T(4,128)(2,1)}, u32[]{:S(2)}, u32[]{:S(2)}) async-start(bf16[16,4,14336]{2,1,0:T(4,128)(2,1)} %select_select_fusion), calls=%async_computation.3 | async-start | bytes 3670016 | tf_op jit(solution)/shard_map/all_to_all | solution.py:131
  394.1 28.2 %all-to-all-done.2 = bf16[16,4,14336]{2,1,0:T(4,128)(2,1)} async-done(((bf16[16,4,14336]{2,1,0:T(4,128)(2,1)}), bf16[16,4,14336]{2,1,0:T(4,128)(2,1)}, u32[]{:S(2)}, u32[]{:S(2)}) %all-to-all-start.2) | async-done | bytes 1835040 | tf_op jit(solution)/shard_map/all_to_all | solution.py:131
  422.2 3.9 reshape.334
  426.1 3.6 convolution_convert_fusion
  429.7 6.8 %reshape.335 = bf16[64,16,2,448]{3,2,1,0:T(2,128)(2,1)} reshape(bf16[64,14336]{1,0:T(8,128)(2,1)} %convolution_convert_fusion) | data formatting | bytes 3670016 | tf_op jit(solution)/shard_map/reshape | solution.py:142
  436.5 7.3 %reduce-scatter.2.cloned.1.call-done = bf16[128,3584]{1,0:T(8,128)(2,1)} async-done(((bf16[1024,3584]{1,0:T(8,128)(2,1)}), bf16[128,3584]{1,0:T(8,128)(2,1)}) %reduce-scatter.2.cloned.1.call-update) | async-done | bytes 917520 | tf_op jit(solution)/shard_map/reduce_scatter | solution.py:101
  (63 shorter events, 26.5 us)
Async XLA Ops:
  7.2 324.6 %copy-start = (bf16[448,3584]{1,0:T(8,128)(2,1)S(1)}, bf16[448,3584]{1,0:T(8,128)(2,1)}, u32[]{:S(2)}) copy-start(bf16[448,3584]{1,0:T(8,128)(2,1)} %param.20) | copy-start | bytes 9633796
  7.2 266.9 %all-gather.6.cloned.1.call-start = ((), (), s32[]{:S(2)}) async-start(), calls=%async_computation.5 | async-start | bytes 7798784 | tf_op jit(solution)/shard_map/all_gather | solution.py:71
  7.9 281.6 %all-gather.8.cloned.1.call-start = ((), (), s32[]{:S(2)}) async-start(), calls=%async_computation.6 | async-start | bytes 7798784 | tf_op jit(solution)/shard_map/all_gather | solution.py:72
  12.6 1.2 copy-start.1
  19.2 8.5 %copy-start.4 = (s32[1024]{0:T(1024)S(1)}, s32[1024]{0:T(1024)}, u32[]{:S(2)}) copy-start(s32[1024]{0:T(1024)} %param.21) | copy-start | bytes 12292
  19.2 254.9 %all-to-all-start = ((bf16[8,128,7168]{2,1,0:T(8,128)(2,1)}), bf16[8,128,7168]{2,1,0:T(8,128)(2,1)}, u32[]{:S(2)}, u32[]{:S(2)}) async-start(bf16[8,128,7168]{2,1,0:T(8,128)(2,1)} %stack.8), calls=%async_computation | async-start | bytes 29360128 | tf_op jit(solution)/shard_map/all_to_all | solution.py:63
  26.2 287.1 %all-gather.4.cloned.1.call-start = ((), (), s32[]{:S(2)}) async-start(), calls=%async_computation.4 | async-start | bytes 7798784 | tf_op jit(solution)/shard_map/all_gather | solution.py:73
  27.0 416.8 %reduce-scatter.2.cloned.1.call-start = ((), (), s32[]{:S(2)}) async-start(), calls=%async_computation.7 | async-start | bytes 8257536 | tf_op jit(solution)/shard_map/reduce_scatter | solution.py:101
  27.7 4.4 copy-start.5
  27.7 239.3 %copy-start.3 = (bf16[3,128,448]{1,2,0:T(8,128)(2,1)S(1)}, bf16[3,128,448]{1,2,0:T(8,128)(2,1)}, u32[]{:S(2)}) copy-start(bf16[3,128,448]{1,2,0:T(8,128)(2,1)} %param.19) | copy-start | bytes 1032196
  267.0 4.9 %slice-start = ((s32[1024]{0:T(1024)}), s32[512]{0:T(512)S(1)}, s32[]{:S(2)}) async-start(s32[1024]{0:T(1024)} %copy-done.5), calls=%async_computation.8 | async-start | bytes 4096 | tf_op jit(solution)/shard_map/slice | solution.py:26
  326.8 3.5 copy-start.2
  326.8 4.0 copy-start.7
  337.9 0.7 copy-start.6
  339.1 46.5 %all-to-all-start.1 = ((s32[16,1,4]{2,1,0:T(1,128)}), s32[16,1,4]{2,1,0:T(1,128)S(1)}, u32[]{:S(2)}, u32[]{:S(2)}) async-start(s32[16,1,4]{2,1,0:T(1,128)} %broadcast_in_dim.104), calls=%async_computation.2 | async-start | bytes 16384 | tf_op jit(solution)/shard_map/all_to_all | solution.py:132
  385.6 36.6 %all-to-all-start.2 = ((bf16[16,4,14336]{2,1,0:T(4,128)(2,1)}), bf16[16,4,14336]{2,1,0:T(4,128)(2,1)}, u32[]{:S(2)}, u32[]{:S(2)}) async-start(bf16[16,4,14336]{2,1,0:T(4,128)(2,1)} %select_select_fusion), calls=%async_computation.3 | async-start | bytes 3670016 | tf_op jit(solution)/shard_map/all_to_all | solution.py:131
Sparse Core Ops, SparseCore 0:
  10.4 92.6 all-gather.5
  105.4 89.2 all-gather.7
  197.2 79.7 all-gather.3
  338.0 105.6 reduce-scatter.1
